TPU v7x, 32 devices: a whole 2x2x4 slice. The times are simulated.
32 devices in a mesh: seq: 8 (over z, core), tp: 4 (over y, x).
Axes of the slice: x: 2, y: 2, z: 4, core: 2. Of those that a mesh axis runs over, the one named last changes fastest.
Arguments:
- tokens: bfloat16 [8, 512, 2048], P('seq', None, 'tp'), may hold values from -6 to 6
- segment_ids: int32 [8, 512], P('seq'), may hold values from 0 to 15, as said below
- shard_map: int32 [32], replicated, may hold values from 0 to 31, each once
- trainer_qkv: float32 [2, 2048, 6144], P(None, ('seq', 'tp')), may hold values from -0.125 to 0.125
- trainer_up: float32 [2, 2048, 8192], P(None, ('seq', 'tp')), may hold values from -0.125 to 0.125
- qkv_bias: bfloat16 [2, 6144], P(None, 'tp'), may hold values from -4 to 4
- up_bias: bfloat16 [2, 8192], P(None, 'tp'), may hold values from -3 to 3
- dense_w: bfloat16 [2, 2048, 2048], P(None, 'tp'), may hold values from -0.125 to 0.125
- down_w: bfloat16 [2, 8192, 2048], P(None, 'tp'), may hold values from -0.0625 to 0.0625
- out_bias: float32 [2, 2048], P(None, 'tp'), may hold values from -3 to 3
- norm_gain: float32 [2, 2, 2048], replicated, may hold values from 0.1 to 1.9
- norm_shift: float32 [2, 2, 2048], replicated, may hold values from -3 to 3
Outputs:
- result: bfloat16 [8, 512, 2048], P('seq', None, 'tp')
Inputs may be any that keep to these rules, and one draw needn't show every extreme that they name: `shard_map`: each trainer shard number appears exactly once. `segment_ids`: along a row the numbers start at 0 and rise by 0 or 1 from token to token; a row holds one prompt of 512 tokens or several packed prompts.
All inputs are finite; a program needn't handle non-finite values.
Results may differ from a plain program's by a relative error of at most 0.015.
Values may be sent and summed in bfloat16 or wider, within the bound.
No kernel may reach another device: no remote copies, remote signals or barrier semaphores. Data moves between devices by JAX's collectives and lax.ppermute only.
A program may use at most 192 MiB of HBM per device.

v0:
```python
import jax
import jax.numpy as jnp
from jax import lax
from jax.sharding import PartitionSpec as P

HD = 256
ROT = 64
LAYERS = 2


def layer_norm(values, gain, shift):
    mean = jnp.mean(values, axis=-1, keepdims=True)
    centred = values - mean
    var = jnp.mean(centred * centred, axis=-1, keepdims=True)
    return centred * lax.rsqrt(var + 1e-05) * gain + shift


def positions(segs):
    length = segs.shape[-1]
    index = jnp.broadcast_to(jnp.arange(length, dtype=jnp.int32), segs.shape)
    first = jnp.ones(segs.shape[:-1] + (1,), dtype=bool)
    flag = jnp.concatenate([first, segs[..., 1:] != segs[..., :-1]], axis=-1)
    start = lax.cummax(jnp.where(flag, index, 0), axis=segs.ndim - 1)
    return index - start


def rotate(values, pos):
    half = ROT // 2
    inverse = 10000.0 ** (-(jnp.arange(half, dtype=jnp.float32) * 2.0 / ROT))
    angle = pos[..., None].astype(jnp.float32) * inverse
    cosine = jnp.cos(angle)[..., None, :]
    sine = jnp.sin(angle)[..., None, :]
    first = values[..., :half]
    second = values[..., half:ROT]
    return jnp.concatenate(
        [first * cosine - second * sine, second * cosine + first * sine, values[..., ROT:]], axis=-1
    )


def shards(
    tokens,
    segment_ids,
    shard_map,
    trainer_qkv,
    trainer_up,
    qkv_bias,
    up_bias,
    dense_w,
    down_w,
    out_bias,
    norm_gain,
    norm_shift,
):
    n_tp = lax.axis_size("tp")
    rows, length, _ = tokens.shape
    block = trainer_qkv.shape[1]
    full_width = block * n_tp * lax.axis_size("seq")
    n_blocks = full_width // block
    heads_here = qkv_bias.shape[1] // (3 * HD)
    qkv_cols = qkv_bias.shape[1]
    wq = trainer_qkv.astype(jnp.bfloat16).reshape(LAYERS, block, n_tp, qkv_cols)
    wu = trainer_up.astype(jnp.bfloat16).reshape(LAYERS, block, n_tp, up_bias.shape[1])
    width_here = tokens.shape[2]

    def exchange(x):
        return lax.all_to_all(x, "tp", split_axis=0, concat_axis=0, tiled=True)

    def spread(local):
        return jnp.broadcast_to(
            local.reshape(1, rows * length, width_here), (n_tp, rows * length, width_here)
        )

    def joined(got):
        return got.transpose(1, 0, 2).reshape(rows, length, n_tp * width_here)

    gathered = []
    for layer in range(LAYERS):
        parts = []
        for part in (wq[layer], wu[layer]):
            part = lax.all_to_all(part, "tp", split_axis=1, concat_axis=0, tiled=True)
            parts.append(lax.all_gather(part.reshape(n_tp * block, -1), "seq", axis=0, tiled=True))
        gathered.append(parts)
    whole = joined(exchange(spread(tokens)))
    pos = positions(segment_ids)
    index = jnp.arange(length, dtype=jnp.int32)
    mask = (index[None, :] <= index[:, None])[None] & (
        segment_ids[:, :, None] == segment_ids[:, None, :]
    )
    mask = mask[:, None]
    stream = tokens
    for layer in range(LAYERS):
        qkv_mat, up_mat = gathered[layer]
        if layer > 0:
            whole = joined(exchange(spread(stream)))
        permuted = jnp.take(whole.reshape(rows, length, n_blocks, block), shard_map, axis=2)
        permuted = permuted.reshape(rows * length, full_width).astype(jnp.float32)

        def norm_of(i):
            gain = jnp.take(norm_gain[layer, i].reshape(n_blocks, block), shard_map, axis=0)
            shift = jnp.take(norm_shift[layer, i].reshape(n_blocks, block), shard_map, axis=0)
            return layer_norm(permuted, gain.reshape(-1), shift.reshape(-1)).astype(jnp.bfloat16)

        attn_in = norm_of(0)
        mlp_in = norm_of(1)
        qkv = jnp.dot(attn_in, qkv_mat, preferred_element_type=jnp.float32) + qkv_bias[
            layer
        ].astype(jnp.float32)
        qkv = qkv.reshape(rows, length, heads_here, 3, HD)
        query = rotate(qkv[:, :, :, 0], pos).astype(jnp.bfloat16)
        keys = rotate(qkv[:, :, :, 1], pos).astype(jnp.bfloat16)
        vals = qkv[:, :, :, 2].astype(jnp.bfloat16)
        scores = jnp.einsum(
            "rqhd,rkhd->rhqk", query, keys, preferred_element_type=jnp.float32
        ) / jnp.sqrt(jnp.float32(HD))
        scores = jnp.where(mask, scores, -jnp.inf)
        probs = jax.nn.softmax(scores, axis=-1).astype(jnp.bfloat16)
        ctx = jnp.einsum("rhqk,rkhd->rqhd", probs, vals, preferred_element_type=jnp.float32).astype(
            jnp.bfloat16
        )
        ctx = ctx.reshape(rows * length, heads_here * HD)
        up = jnp.dot(mlp_in, up_mat, preferred_element_type=jnp.float32) + up_bias[layer].astype(
            jnp.float32
        )
        hidden_units = jax.nn.gelu(up, approximate=False).astype(jnp.bfloat16)
        partial_terms = jnp.dot(ctx, dense_w[layer], preferred_element_type=jnp.float32) + jnp.dot(
            hidden_units, down_w[layer], preferred_element_type=jnp.float32
        )
        partial_terms = partial_terms.astype(jnp.bfloat16)
        split = partial_terms.reshape(rows * length, n_tp, width_here).transpose(1, 0, 2)
        summed = jnp.sum(exchange(split).astype(jnp.float32), axis=0)
        flat_stream = stream.astype(jnp.float32).reshape(rows * length, -1)
        stream = (
            (flat_stream + summed + out_bias[layer]).astype(jnp.bfloat16).reshape(rows, length, -1)
        )
    return stream


def solution(mesh):
    in_specs = (
        P("seq", None, "tp"),
        P("seq", None),
        P(),
        P(None, ("seq", "tp"), None),
        P(None, ("seq", "tp"), None),
        P(None, "tp"),
        P(None, "tp"),
        P(None, "tp", None),
        P(None, "tp", None),
        P(None, "tp"),
        P(),
        P(),
    )
    out_specs = P("seq", None, "tp")
    return jax.shard_map(shards, mesh=mesh, in_specs=in_specs, out_specs=out_specs, check_vma=False)
```

profile of v0, /device:TPU:0, one launch (start us, length us, event | category | flops | bytes accessed | tf_op | source)
XLA Modules:
  0.0 388.9 jit_solution(17570129192269081183)
XLA Ops:
  6.5 2.1 convert_element_type.153
  10.4 16.4 %all_to_all.80 = bf16[64,4,1536]{2,0,1:T(8,128)(2,1)} all-to-all(bf16[64,4,1536]{2,0,1:T(8,128)(2,1)S(1)} %copy.48), channel_id=1, replica_groups=mesh['seq'=8,'tp'=4] {'tp'}, dimensions={1} | all-to-all | bytes 1572864 | tf_op jit(solution)/shard_map/all_to_all | solution.py:80
  26.8 2.4 convert_element_type.161
  30.9 16.0 %all_to_all.81 = bf16[64,4,2048]{2,0,1:T(8,128)(2,1)} all-to-all(bf16[64,4,2048]{2,0,1:T(8,128)(2,1)S(1)} %copy.54), channel_id=1, replica_groups=mesh['seq'=8,'tp'=4] {'tp'}, dimensions={1} | all-to-all | bytes 2097152 | tf_op jit(solution)/shard_map/all_to_all | solution.py:80
  47.7 12.1 %all_to_all.82 = bf16[64,4,1536]{2,0,1:T(8,128)(2,1)} all-to-all(bf16[64,4,1536]{2,0,1:T(8,128)(2,1)S(1)} %copy.57), channel_id=1, replica_groups=mesh['seq'=8,'tp'=4] {'tp'}, dimensions={1} | all-to-all | bytes 1572864 | tf_op jit(solution)/shard_map/all_to_all | solution.py:80
  60.6 1.6 copy.63
  62.2 3.5 all-to-all-start.6
  73.6 2.1 all-to-all-done.6
  75.7 1.6 broadcast_in_dim.47
  77.4 3.6 all-to-all-start
  82.4 1.7 multiply_cosine_fusion
  84.2 17.2 %all-to-all-done = bf16[4,512,512]{1,2,0:T(8,128)(2,1)S(1)} async-done(((bf16[4,512,512]{1,2,0:T(8,128)(2,1)}), bf16[4,512,512]{1,2,0:T(8,128)(2,1)S(1)}, u32[]{:S(2)}, u32[]{:S(2)}) %all-to-all-start) | async-done | bytes 2097184 | tf_op jit(solution)/shard_map/all_to_all | solution.py:66
  102.7 2.3 gather_fusion
  106.7 2.8 add_convert_fusion.5
  109.4 8.6 %convolution_add_fusion.1 = f32[512,1536]{1,0:T(8,128)} fusion(bf16[512,2048]{0,1:T(8,128)(2,1)} %get-tuple-element.23, bf16[2048,1536]{1,0:T(8,128)(2,1)} %all-gather.5.cloned.1.call-done, f32[1536]{0:T(1024)S(1)} %get-tuple-element.16), kind=kOutput, calls=%fused_computation.73 | convolution fusion | flops 3222011904 | bytes 11540480 | tf_op jit(solution)/shard_map/dot_general | solution.py:105
  118.1 2.9 copy.49
  121.0 1.5 fusion.182
  122.5 2.6 copy.67
  125.1 2.5 copy.68
  127.6 2.3 fusion.47
  130.0 2.3 fusion.48
  132.2 3.1 fusion.79
  135.3 4.4 %fusion.186 = (f32[2,512]{1,0:T(2,128)S(1)}, f32[2,512,512]{1,2,0:T(8,128)}) fusion(pred[512,512]{0,1:T(8,128)(4,1)} %fusion.44, bf16[512,2,192]{2,0,1:T(8,128)(2,1)} %fusion.48, bf16[512,2,32]{2,0,1:T(8,128)(2,1)} %get-tuple-element.34, bf16[512,2,32]{2,0,1:T(8,128)(2,1)} %get-tuple-element.33, bf16[512,2,192]{2,0,1:T(8,128)(2,1)} %fusion.47, ...), kind=kOutput, calls=%fused_computation.267 | convolution fusion | flops 273678848 | bytes 3411968 | tf_op jit(solution)/shard_map/sub | solution.py:116
  139.7 2.9 convolution_convert_fusion.1
  142.6 31.1 %all-gather.7.cloned.1.call-done = bf16[2048,2048]{1,0:T(8,128)(2,1)} async-done(((bf16[256,2048]{1,0:T(8,128)(2,1)}), bf16[2048,2048]{1,0:T(8,128)(2,1)}) %all-gather.7.cloned.1.call-update) | async-done | bytes 8388624 | tf_op jit(solution)/shard_map/all_gather | solution.py:81
  173.8 26.3 %fusion.4 = f32[512,2048]{1,0:T(8,128)} fusion(bf16[2,2048,2048]{2,1,0:T(8,128)(2,1)} %param.24, bf16[512,2048]{0,1:T(8,128)(2,1)} %get-tuple-element.24, bf16[2048,2048]{1,0:T(8,128)(2,1)} %all-gather.7.cloned.1.call-done, f32[2048]{0:T(1024)S(1)} %bitcast.214), kind=kOutput, calls=%fused_computation.14 | convolution fusion | flops 8659140608 | bytes 23076864 | tf_op jit(solution)/shard_map/dot_general | solution.py:125
  200.1 4.2 %add_convert_fusion.3 = bf16[512,2048]{1,0:T(8,128)(2,1)S(1)} fusion(f32[512,2048]{1,0:T(8,128)} %fusion.4, bf16[512,512]{0,1:T(8,128)(2,1)S(1)} %bitcast.208, bf16[2,512,2048]{2,1,0:T(8,128)(2,1)} %param.23), kind=kOutput, calls=%fused_computation.49 | convolution fusion | flops 1075838976 | bytes 8912896 | tf_op jit(solution)/shard_map/dot_general | solution.py:125
  204.3 1.6 copy.86
  205.8 3.8 all-to-all-start.3
  209.7 25.4 %all-to-all-done.3 = bf16[4,512,512]{2,1,0:T(8,128)(2,1)S(1)} async-done(((bf16[4,512,512]{2,1,0:T(8,128)(2,1)}), bf16[4,512,512]{2,1,0:T(8,128)(2,1)S(1)}, u32[]{:S(2)}, u32[]{:S(2)}) %all-to-all-start.3) | async-done | bytes 2097184 | tf_op jit(solution)/shard_map/all_to_all | solution.py:66
  235.8 1.6 broadcast_in_dim.52
  237.4 3.6 all-to-all-start.4
  241.3 24.4 %all-to-all-done.4 = bf16[4,512,512]{1,2,0:T(8,128)(2,1)S(1)} async-done(((bf16[4,512,512]{1,2,0:T(8,128)(2,1)}), bf16[4,512,512]{1,2,0:T(8,128)(2,1)S(1)}, u32[]{:S(2)}, u32[]{:S(2)}) %all-to-all-start.4) | async-done | bytes 2097184 | tf_op jit(solution)/shard_map/all_to_all | solution.py:66
  267.0 2.3 gather_fusion.5
  271.0 2.8 add_convert_fusion.2
  273.8 8.8 %convolution_add_fusion = f32[512,1536]{1,0:T(8,128)} fusion(bf16[512,2048]{0,1:T(8,128)(2,1)} %get-tuple-element.21, bf16[2048,1536]{1,0:T(8,128)(2,1)} %all-gather.9.cloned.1.call-done, f32[1536]{0:T(1024)S(1)} %get-tuple-element.15), kind=kOutput, calls=%fused_computation.72 | convolution fusion | flops 3222011904 | bytes 11540480 | tf_op jit(solution)/shard_map/dot_general | solution.py:105
  282.5 2.8 copy.58
  286.8 2.6 copy.69
  289.5 2.5 copy.70
  292.0 2.3 fusion.49
  294.3 2.2 fusion.50
  296.5 3.2 fusion.83
  299.7 4.5 %fusion.191 = (f32[2,512]{1,0:T(2,128)S(1)}, f32[2,512,512]{1,2,0:T(8,128)}) fusion(pred[512,512]{0,1:T(8,128)(4,1)} %fusion.44, bf16[512,2,192]{2,0,1:T(8,128)(2,1)} %fusion.50, bf16[512,2,32]{2,0,1:T(8,128)(2,1)} %get-tuple-element.28, bf16[512,2,32]{2,0,1:T(8,128)(2,1)} %get-tuple-element.27, bf16[512,2,192]{2,0,1:T(8,128)(2,1)} %fusion.49, ...), kind=kOutput, calls=%fused_computation.268 | convolution fusion | flops 273678848 | bytes 3411968 | tf_op jit(solution)/shard_map/sub | solution.py:116
  304.2 2.9 convolution_convert_fusion
  307.0 13.9 %all-gather.11.cloned.1.call-done = bf16[2048,2048]{1,0:T(8,128)(2,1)} async-done(((bf16[256,2048]{1,0:T(8,128)(2,1)}), bf16[2048,2048]{1,0:T(8,128)(2,1)}) %all-gather.11.cloned.1.call-update) | async-done | bytes 8388624 | tf_op jit(solution)/shard_map/all_gather | solution.py:81
  321.0 26.2 %fusion.2 = f32[512,2048]{1,0:T(8,128)} fusion(bf16[2,2048,2048]{2,1,0:T(8,128)(2,1)} %param.24, bf16[512,2048]{0,1:T(8,128)(2,1)} %get-tuple-element.22, bf16[2048,2048]{1,0:T(8,128)(2,1)} %all-gather.11.cloned.1.call-done, f32[2048]{0:T(1024)S(1)} %bitcast.213), kind=kOutput, calls=%fused_computation.12 | convolution fusion | flops 8659140608 | bytes 23076864 | tf_op jit(solution)/shard_map/dot_general | solution.py:125
  347.2 4.1 %add_convert_fusion = bf16[512,2048]{1,0:T(8,128)(2,1)S(1)} fusion(f32[512,2048]{1,0:T(8,128)} %fusion.2, bf16[512,512]{0,1:T(8,128)(2,1)S(1)} %bitcast.207, bf16[2,512,2048]{2,1,0:T(8,128)(2,1)} %param.23), kind=kOutput, calls=%fused_computation.31 | convolution fusion | flops 1075838976 | bytes 8912896 | tf_op jit(solution)/shard_map/dot_general | solution.py:125
  351.5 29.4 %all_to_all.83 = bf16[4,512,512]{2,1,0:T(8,128)(2,1)S(1)} all-to-all(bf16[4,512,512]{2,1,0:T(8,128)(2,1)S(1)} %bitcast.192), channel_id=1, replica_groups=mesh['seq'=8,'tp'=4] {'tp'}, dimensions={0} | all-to-all | bytes 4194304 | tf_op jit(solution)/shard_map/all_to_all | solution.py:66
  (110 shorter events, 24.3 us)
Async XLA Ops:
  6.5 102.9 %all-gather.5.cloned.1.call-start = ((), (), s32[]{:S(2)}) async-start(), calls=%async_computation.8 | async-start | bytes 7077888 | tf_op jit(solution)/shard_map/all_gather | solution.py:81
  26.8 147.0 %all-gather.7.cloned.1.call-start = ((), (), s32[]{:S(2)}) async-start(), calls=%async_computation.9 | async-start | bytes 9437184 | tf_op jit(solution)/shard_map/all_gather | solution.py:81
  30.3 16.7 %copy-start.5 = (bf16[1,64,6144]{2,1,0:T(8,128)(2,1)S(1)}, bf16[1,64,6144]{2,1,0:T(8,128)(2,1)}, u32[]{:S(2)}) copy-start(bf16[1,64,6144]{2,1,0:T(8,128)(2,1)} %get-tuple-element.31) | copy-start | bytes 2359300
  46.9 226.8 %all-gather.9.cloned.1.call-start = ((), (), s32[]{:S(2)}) async-start(), calls=%async_computation.10 | async-start | bytes 7077888 | tf_op jit(solution)/shard_map/all_gather | solution.py:81
  47.7 18.0 %copy-start.11 = (f32[2,2,2048]{2,1,0:T(2,128)S(1)}, f32[2,2,2048]{2,1,0:T(2,128)}, u32[]{:S(2)}) copy-start(f32[2,2,2048]{2,1,0:T(2,128)} %param.27) | copy-start | bytes 98308
  47.7 18.0 %copy-start.12 = (f32[2,2,2048]{2,1,0:T(2,128)S(1)}, f32[2,2,2048]{2,1,0:T(2,128)}, u32[]{:S(2)}) copy-start(f32[2,2,2048]{2,1,0:T(2,128)} %param.26) | copy-start | bytes 98308
  47.7 18.3 %copy-start.15 = (s32[32]{0:T(128)S(1)}, s32[32]{0:T(128)}, u32[]{:S(2)}) copy-start(s32[32]{0:T(128)} %param.18) | copy-start | bytes 388
  59.8 12.9 %copy-start.9 = (s32[1,512]{1,0:T(1,128)S(1)}, s32[1,512]{1,0:T(1,128)}, u32[]{:S(2)}) copy-start(s32[1,512]{1,0:T(1,128)} %param.17) | copy-start | bytes 6148
  62.2 13.5 %all-to-all-start.6 = ((bf16[64,4,2048]{2,0,1:T(8,128)(2,1)}), bf16[64,4,2048]{2,0,1:T(8,128)(2,1)S(1)}, u32[]{:S(2)}, u32[]{:S(2)}) async-start(bf16[64,4,2048]{2,0,1:T(8,128)(2,1)} %copy.63), calls=%async_computation.6 | async-start | bytes 2097152 | tf_op jit(solution)/shard_map/all_to_all | solution.py:80
  70.5 10.8 %copy-start.13 = (bf16[2,1536]{1,0:T(2,128)(2,1)S(1)}, bf16[2,1536]{1,0:T(2,128)(2,1)}, u32[]{:S(2)}) copy-start(bf16[2,1536]{1,0:T(2,128)(2,1)} %param.21) | copy-start | bytes 18436
  71.5 12.7 %copy-start.10 = (bf16[2,2048]{1,0:T(2,128)(2,1)S(1)}, bf16[2,2048]{1,0:T(2,128)(2,1)}, u32[]{:S(2)}) copy-start(bf16[2,2048]{1,0:T(2,128)(2,1)} %param.22) | copy-start | bytes 24580
  75.7 8.4 %copy-start.4 = (bf16[64,4,2048]{2,0,1:T(8,128)(2,1)}, bf16[64,4,2048]{2,0,1:T(8,128)(2,1)S(1)}, u32[]{:S(2)}) copy-start(bf16[64,4,2048]{2,0,1:T(8,128)(2,1)S(1)} %all-to-all-done.6) | copy-start | bytes 3145732
  77.4 24.0 %all-to-all-start = ((bf16[4,512,512]{1,2,0:T(8,128)(2,1)}), bf16[4,512,512]{1,2,0:T(8,128)(2,1)S(1)}, u32[]{:S(2)}, u32[]{:S(2)}) async-start(bf16[4,512,512]{1,2,0:T(8,128)(2,1)} %broadcast_in_dim.47), calls=%async_computation | async-start | bytes 4194304 | tf_op jit(solution)/shard_map/all_to_all | solution.py:66
  81.0 240.0 %all-gather.11.cloned.1.call-start = ((), (), s32[]{:S(2)}) async-start(), calls=%async_computation.11 | async-start | bytes 9437184 | tf_op jit(solution)/shard_map/all_gather | solution.py:81
  101.3 1.4 copy-start
  173.8 26.3 %copy-start.8 = (bf16[2,256,512]{2,1,0:T(8,128)(2,1)S(1)}, bf16[2,256,512]{2,1,0:T(8,128)(2,1)}, u32[]{:S(2)}) copy-start(bf16[2,256,512]{2,1,0:T(8,128)(2,1)} %convolution_convert_fusion.1) | copy-start | bytes 1572868
  204.3 5.4 %copy-start.14 = (f32[2,512]{1,0:T(2,128)S(1)}, f32[2,512]{1,0:T(2,128)}, u32[]{:S(2)}) copy-start(f32[2,512]{1,0:T(2,128)} %param.25) | copy-start | bytes 12292
  205.8 29.6 %copy-start.6 = (bf16[1,512,512]{2,1,0:T(8,128)(2,1)S(1)}, bf16[1,512,512]{2,1,0:T(8,128)(2,1)}, u32[]{:S(2)}) copy-start(bf16[1,512,512]{2,1,0:T(8,128)(2,1)} %param.16) | copy-start | bytes 1572868
  205.8 29.2 %all-to-all-start.3 = ((bf16[4,512,512]{2,1,0:T(8,128)(2,1)}), bf16[4,512,512]{2,1,0:T(8,128)(2,1)S(1)}, u32[]{:S(2)}, u32[]{:S(2)}) async-start(bf16[4,512,512]{2,1,0:T(8,128)(2,1)} %bitcast.191), calls=%async_computation.3 | async-start | bytes 4194304 | tf_op jit(solution)/shard_map/all_to_all | solution.py:66
  235.6 1.8 copy-start.2
  237.4 28.3 %all-to-all-start.4 = ((bf16[4,512,512]{1,2,0:T(8,128)(2,1)}), bf16[4,512,512]{1,2,0:T(8,128)(2,1)S(1)}, u32[]{:S(2)}, u32[]{:S(2)}) async-start(bf16[4,512,512]{1,2,0:T(8,128)(2,1)} %broadcast_in_dim.52), calls=%async_computation.4 | async-start | bytes 4194304 | tf_op jit(solution)/shard_map/all_to_all | solution.py:66
  265.6 1.4 copy-start.1
  321.0 26.2 %copy-start.7 = (bf16[2,256,512]{2,1,0:T(8,128)(2,1)S(1)}, bf16[2,256,512]{2,1,0:T(8,128)(2,1)}, u32[]{:S(2)}) copy-start(bf16[2,256,512]{2,1,0:T(8,128)(2,1)} %convolution_convert_fusion) | copy-start | bytes 1572868
  351.5 29.8 %copy-start.3 = (bf16[1,512,512]{2,1,0:T(8,128)(2,1)S(1)}, bf16[1,512,512]{2,1,0:T(8,128)(2,1)}, u32[]{:S(2)}) copy-start(bf16[1,512,512]{2,1,0:T(8,128)(2,1)} %copy-done.2) | copy-start | bytes 1572868
Sparse Core Ops, SparseCore 0:
  26.9 64.4 all-gather.4
  93.0 80.6 all-gather.6
  175.4 63.2 all-gather.8
  240.2 80.7 all-gather.10
where the time goes:
time: 395 us; the launch traced here: 389 us
  waiting for transfers between devices  114 us (29%)
  matrix products  92.9 us (24%)
  blocking collectives  73.9 us (19%)
  local copies, waits for them, and re-layouts  54.4 us (14%)
  other arithmetic  24.9 us (6%)
  starting transfers between devices  15 us (4%)
  between operations  13.7 us (3%)
    all_to_all x3, waiting for transfers between devices, exchange(): return lax.all_to_all(x, 'tp', split_axis=0, concat_axis=0, tiled=True)  66.9 us
    dot_general x2, matrix products, shards(): jnp.dot(hidden_units, down_w[layer], preferred_element_type=jnp.float32)  52.6 us
    all_gather x4, waiting for transfers between devices, shards(): lax.all_gather(part.reshape(n_tp * block, -1), 'seq', axis=0, tiled=True)  45.1 us
    all_to_all x3, blocking collectives, shards(): part = lax.all_to_all(part, 'tp', split_axis=1, concat_axis=0, tiled=True)  44.5 us
    all_to_all x1, blocking collectives, exchange(): return lax.all_to_all(x, 'tp', split_axis=0, concat_axis=0, tiled=True)  29.4 us
    dot_general x2, matrix products, shards(): jnp.dot(attn_in, qkv_mat, preferred_element_type=jnp.float32)  17.4 us
    unnamed x36, local copies, waits for them, and re-layouts  13.1 us
    all_to_all x3, starting transfers between devices, exchange(): return lax.all_to_all(x, 'tp', split_axis=0, concat_axis=0, tiled=True)  11 us
  transfers between devices with their start and end apart: 8, of which 6 were waited for; matrix products, arithmetic and copies ran while one was open for 34% of the time, Pallas kernels for 0%

commit v1 on v0

--- a/solution.py
+++ b/solution.py
@@ -1,3 +1,4 @@
+import functools
 import jax
 import jax.numpy as jnp
 from jax import lax
@@ -6,6 +7,35 @@
 HD = 256
 ROT = 64
 LAYERS = 2
+
+
+def change_group(load, which_dim):
+    x_new = list(load.shape[1:])
+    x_new[which_dim] *= load.shape[0]
+    return jnp.moveaxis(load, 0, which_dim).reshape(x_new)
+
+
+def tell_the_records(raw, named_axis, in_dim):
+    width = lax.axis_size(named_axis)
+    store = tuple(((m, (m + 1) % width) for m in range(width)))
+    table = tuple(((s, no) for no, s in store))
+    small, res = ([], [])
+    for dev in range(width - 1):
+        if dev % 2 == 0:
+            before = lax.ppermute(small[-1] if small else raw, named_axis, store)
+            small.append(before)
+        else:
+            piece_out = lax.ppermute(res[-1] if res else raw, named_axis, table)
+            res.append(piece_out)
+    inter = jnp.stack([*small[::-1], raw, *res], 0)
+    val2 = lax.axis_index(named_axis)
+    state_now = len(small)
+    seen_now = val2 - state_now
+    inter = inter[(jnp.arange(width) - seen_now) % width]
+    return change_group(inter, in_dim)
+
+
+_resolve_table = functools.partial(tell_the_records, named_axis="seq", in_dim=0)
 
 
 def layer_norm(values, gain, shift):
@@ -78,7 +108,7 @@
         parts = []
         for part in (wq[layer], wu[layer]):
             part = lax.all_to_all(part, "tp", split_axis=1, concat_axis=0, tiled=True)
-            parts.append(lax.all_gather(part.reshape(n_tp * block, -1), "seq", axis=0, tiled=True))
+            parts.append(_resolve_table(part.reshape(n_tp * block, -1)))
         gathered.append(parts)
     whole = joined(exchange(spread(tokens)))
     pos = positions(segment_ids)

time: 395 us -> 552 us (1.40)
  the two profiles are of different devices: /device:TPU:0 before, /device:TPU:24 now
where the time goes in v1:
time: 552 us; the launch traced here: 541 us
  waiting for transfers between devices  177 us (32%)
  local copies, waits for them, and re-layouts  151 us (27%)
  matrix products  90.8 us (16%)
  starting transfers between devices  67 us (12%)
  blocking collectives  28.5 us (5%)
  other arithmetic  26.7 us (5%)
    ppermute x16, waiting for transfers between devices, tell_the_records(): before = lax.ppermute(small[-1] if small else raw, named_axis, store)  82.6 us
    unnamed x86, local copies, waits for them, and re-layouts  67.9 us
    dot_general x2, matrix products, shards(): jnp.dot(hidden_units, down_w[layer], preferred_element_type=jnp.float32)  51.9 us
    ppermute x12, waiting for transfers between devices, tell_the_records(): piece_out = lax.ppermute(res[-1] if res else raw, named_axis, table)  51.5 us
    ppermute x16, starting transfers between devices, tell_the_records(): before = lax.ppermute(small[-1] if small else raw, named_axis, store)  30 us
    gather x4, local copies, waits for them, and re-layouts, tell_the_records(): inter = inter[(jnp.arange(width) - seen_now) % width]  29.6 us
    all_to_all x3, waiting for transfers between devices, exchange(): return lax.all_to_all(x, 'tp', split_axis=0, concat_axis=0, tiled=True)  28.6 us
    all_to_all x1, blocking collectives, exchange(): return lax.all_to_all(x, 'tp', split_axis=0, concat_axis=0, tiled=True)  28.5 us
  transfers between devices with their start and end apart: 35, of which 16 were waited for; matrix products, arithmetic and copies ran while one was open for 36% of the time, Pallas kernels for 0%

profile of v1, /device:TPU:24, one launch (start us, length us, event | category | flops | bytes accessed | tf_op | source)
XLA Modules:
  0.0 541.4 jit_solution(1579487758090627688)
XLA Ops:
  4.7 4.2 all-to-all-start.1
  20.1 3.5 all-to-all-start.5
  24.9 9.0 %all-to-all-done.5 = bf16[64,4,1536]{2,0,1:T(8,128)(2,1)S(1)} async-done(((bf16[64,4,1536]{2,0,1:T(8,128)(2,1)}), bf16[64,4,1536]{2,0,1:T(8,128)(2,1)S(1)}, u32[]{:S(2)}, u32[]{:S(2)}) %all-to-all-start.5) | async-done | bytes 786464 | tf_op jit(solution)/shard_map/all_to_all | solution.py:110
  33.9 3.5 all-to-all-start.2
  46.5 3.9 all-to-all-done.2
  50.5 2.9 broadcast_in_dim.43
  53.4 3.6 all-to-all-start
  59.2 10.2 %collective-permute-done.1 = bf16[256,1536]{1,0:T(8,128)(2,1)} collective-permute-done((bf16[256,1536]{1,0:T(8,128)(2,1)}, bf16[256,1536]{1,0:T(8,128)(2,1)}, u32[]{:S(2)}, u32[]{:S(2)}) %collective-permute-start.1) | collective-permute-done | bytes 786464 | tf_op jit(solution)/shard_map/ppermute | solution.py:25
  75.0 3.5 collective-permute-start.7
  78.6 2.8 all-to-all-done
  81.4 4.3 all-to-all-start.6
  91.6 3.3 fusion.17
  94.9 3.8 collective-permute-done.14
  98.7 42.4 %collective-permute-done.3 = bf16[256,1536]{1,0:T(8,128)(2,1)S(1)} collective-permute-done((bf16[256,1536]{1,0:T(8,128)(2,1)}, bf16[256,1536]{1,0:T(8,128)(2,1)S(1)}, u32[]{:S(2)}, u32[]{:S(2)}) %collective-permute-start.3) | collective-permute-done | bytes 786464 | tf_op jit(solution)/shard_map/ppermute | solution.py:25
  141.1 5.7 %collective-permute-start.15 = (bf16[256,1536]{1,0:T(8,128)(2,1)}, bf16[256,1536]{1,0:T(8,128)(2,1)}, u32[]{:S(2)}, u32[]{:S(2)}) collective-permute-start(bf16[256,1536]{1,0:T(8,128)(2,1)} %collective-permute-done.14), channel_id=1, source_target_pairs={{0,4},{4,8},{8,12},{12,16},{16,20},{20,24},{24,28},{28,0},{1,5},{5... | collective-permute-start | bytes 2359304 | tf_op jit(solution)/shard_map/ppermute | solution.py:25
  154.2 4.2 collective-permute-start.21
  164.2 12.3 %collective-permute-done.21 = bf16[256,2048]{1,0:T(8,128)(2,1)} collective-permute-done((bf16[256,2048]{1,0:T(8,128)(2,1)}, bf16[256,2048]{1,0:T(8,128)(2,1)}, u32[]{:S(2)}, u32[]{:S(2)}) %collective-permute-start.21) | collective-permute-done | bytes 1048608 | tf_op jit(solution)/shard_map/ppermute | solution.py:25
  176.5 6.6 %collective-permute-start.8 = (bf16[256,2048]{1,0:T(8,128)(2,1)}, bf16[256,2048]{1,0:T(8,128)(2,1)}, u32[]{:S(2)}, u32[]{:S(2)}) collective-permute-start(bf16[256,2048]{1,0:T(8,128)(2,1)} %collective-permute-done.7), channel_id=1, source_target_pairs={{0,4},{4,8},{8,12},{12,16},{16,20},{20,24},{24,28},{28,0},{1,5},{5... | collective-permute-start | bytes 3145736 | tf_op jit(solution)/shard_map/ppermute | solution.py:25
  184.5 14.7 %collective-permute-done.19 = bf16[256,1536]{1,0:T(8,128)(2,1)S(1)} collective-permute-done((bf16[256,1536]{1,0:T(8,128)(2,1)}, bf16[256,1536]{1,0:T(8,128)(2,1)S(1)}, u32[]{:S(2)}, u32[]{:S(2)}) %collective-permute-start.19) | collective-permute-done | bytes 786464 | tf_op jit(solution)/shard_map/ppermute | solution.py:28
  199.9 16.0 %collective-permute-done.6 = bf16[256,1536]{1,0:T(8,128)(2,1)S(1)} collective-permute-done((bf16[256,1536]{1,0:T(8,128)(2,1)S(1)}, bf16[256,1536]{1,0:T(8,128)(2,1)S(1)}, u32[]{:S(2)}, u32[]{:S(2)}) %collective-permute-start.6) | collective-permute-done | bytes 786464 | tf_op jit(solution)/shard_map/ppermute | solution.py:28
  219.1 6.5 %gather_fusion = bf16[8,256,1536]{2,1,0:T(8,128)(2,1)} fusion(bf16[8,256,1536]{2,1,0:T(8,128)(2,1)} %bitcast_dynamic-update-slice_fusion.21, s32[1024]{0:T(1024)S(1)} %pad_clamp_fusion), kind=kCustom, calls=%fused_computation.10 | custom fusion | bytes 12582944 | tf_op jit(solution)/shard_map/gather | solution.py:34
  225.7 8.0 %convolution_add_fusion.1 = f32[512,1536]{1,0:T(8,128)} fusion(bf16[512,2048]{0,1:T(8,128)(2,1)S(1)} %bitcast.271, bf16[2048,1536]{1,0:T(8,128)(2,1)} %bitcast.262, f32[1536]{0:T(1024)S(1)} %copy-done.22), kind=kOutput, calls=%fused_computation.87 | convolution fusion | flops 3222011904 | bytes 11540480 | tf_op jit(solution)/shard_map/dot_general | solution.py:135
  240.7 20.3 %collective-permute-done.26 = bf16[256,2048]{1,0:T(8,128)(2,1)} collective-permute-done((bf16[256,2048]{1,0:T(8,128)(2,1)}, bf16[256,2048]{1,0:T(8,128)(2,1)}, u32[]{:S(2)}, u32[]{:S(2)}) %collective-permute-start.26) | collective-permute-done | bytes 1048608 | tf_op jit(solution)/shard_map/ppermute | solution.py:28
  275.9 2.6 copy.71
  289.8 6.4 %gather_fusion.2 = bf16[8,256,1536]{2,1,0:T(8,128)(2,1)} fusion(bf16[8,256,1536]{2,1,0:T(8,128)(2,1)} %bitcast_dynamic-update-slice_fusion.14, s32[1024]{0:T(1024)S(1)} %pad_clamp_fusion), kind=kCustom, calls=%fused_computation.12 | custom fusion | bytes 12582944 | tf_op jit(solution)/shard_map/gather | solution.py:34
  296.1 3.1 fusion.95
  299.2 4.4 fusion.204
  303.6 2.8 convolution_convert_fusion.1
  306.5 2.9 collective-permute-start.24
  309.4 13.2 %collective-permute-done.10 = bf16[256,2048]{1,0:T(8,128)(2,1)} collective-permute-done((bf16[256,2048]{1,0:T(8,128)(2,1)}, bf16[256,2048]{1,0:T(8,128)(2,1)}, u32[]{:S(2)}, u32[]{:S(2)}) %collective-permute-start.10) | collective-permute-done | bytes 1048608 | tf_op jit(solution)/shard_map/ppermute | solution.py:25
  340.0 8.6 %gather_fusion.1 = bf16[8,256,2048]{2,1,0:T(8,128)(2,1)} fusion(bf16[8,256,2048]{2,1,0:T(8,128)(2,1)} %bitcast_dynamic-update-slice_fusion.7, s32[1024]{0:T(1024)S(1)} %pad_clamp_fusion), kind=kCustom, calls=%fused_computation.11 | custom fusion | bytes 16777248 | tf_op jit(solution)/shard_map/gather | solution.py:34
  348.7 25.6 %fusion.4 = f32[512,2048]{1,0:T(8,128)} fusion(bf16[2,2048,2048]{2,1,0:T(8,128)(2,1)} %param.24, bf16[512,2048]{0,1:T(8,128)(2,1)S(1)} %bitcast.270, bf16[2048,2048]{1,0:T(8,128)(2,1)} %bitcast.248, f32[2048]{0:T(1024)S(1)} %bitcast.282), kind=kOutput, calls=%fused_computation.18 | convolution fusion | flops 8659140608 | bytes 23076864 | tf_op jit(solution)/shard_map/dot_general | solution.py:155
  374.2 4.3 add_convert_fusion.1
  380.0 4.2 all-to-all-start.3
  392.3 17.0 %all-to-all-done.3 = bf16[4,512,512]{2,1,0:T(8,128)(2,1)S(1)} async-done(((bf16[4,512,512]{2,1,0:T(8,128)(2,1)}), bf16[4,512,512]{2,1,0:T(8,128)(2,1)S(1)}, u32[]{:S(2)}, u32[]{:S(2)}) %all-to-all-start.3) | async-done | bytes 2097184 | tf_op jit(solution)/shard_map/all_to_all | solution.py:96
  411.6 3.6 all-to-all-start.4
  424.6 8.1 %gather_fusion.3 = bf16[8,256,2048]{2,1,0:T(8,128)(2,1)} fusion(bf16[8,256,2048]{2,1,0:T(8,128)(2,1)} %bitcast_dynamic-update-slice_fusion, s32[1024]{0:T(1024)S(1)} %pad_clamp_fusion), kind=kCustom, calls=%fused_computation.13 | custom fusion | bytes 16777248 | tf_op jit(solution)/shard_map/gather | solution.py:34
  432.6 8.8 %all-to-all-done.4 = bf16[4,512,512]{1,2,0:T(8,128)(2,1)S(1)} async-done(((bf16[4,512,512]{1,2,0:T(8,128)(2,1)}), bf16[4,512,512]{1,2,0:T(8,128)(2,1)S(1)}, u32[]{:S(2)}, u32[]{:S(2)}) %all-to-all-start.4) | async-done | bytes 2097184 | tf_op jit(solution)/shard_map/all_to_all | solution.py:96
  446.7 2.8 fusion.21
  449.5 8.0 %convolution_add_fusion = f32[512,1536]{1,0:T(8,128)} fusion(bf16[512,2048]{0,1:T(8,128)(2,1)S(1)} %bitcast.273, bf16[2048,1536]{1,0:T(8,128)(2,1)} %bitcast.261, f32[1536]{0:T(1024)S(1)} %copy-done.21), kind=kOutput, calls=%fused_computation.86 | convolution fusion | flops 3222011904 | bytes 11540480 | tf_op jit(solution)/shard_map/dot_general | solution.py:135
  457.5 2.6 copy.62
  461.6 2.6 copy.73
  469.1 3.1 fusion.99
  473.2 4.4 fusion.209
  477.7 2.8 convolution_convert_fusion
  480.5 26.3 %fusion.2 = f32[512,2048]{1,0:T(8,128)} fusion(bf16[2,2048,2048]{2,1,0:T(8,128)(2,1)} %param.24, bf16[512,2048]{0,1:T(8,128)(2,1)} %bitcast.272, bf16[2048,2048]{1,0:T(8,128)(2,1)} %bitcast.247, f32[2048]{0:T(1024)S(1)} %bitcast.281), kind=kOutput, calls=%fused_computation.16 | convolution fusion | flops 8659140608 | bytes 23076864 | tf_op jit(solution)/shard_map/dot_general | solution.py:155
  506.9 4.1 add_convert_fusion
  511.2 28.5 %all_to_all.80 = bf16[4,512,512]{2,1,0:T(8,128)(2,1)S(1)} all-to-all(bf16[4,512,512]{2,1,0:T(8,128)(2,1)S(1)} %bitcast.252), channel_id=1, replica_groups=mesh['seq'=8,'tp'=4] {'tp'}, dimensions={0} | all-to-all | bytes 4194304 | tf_op jit(solution)/shard_map/all_to_all | solution.py:96
  (209 shorter events, 144.5 us)
Async XLA Ops:
  4.7 15.4 %all-to-all-start.1 = ((bf16[64,4,1536]{2,0,1:T(8,128)(2,1)}), bf16[64,4,1536]{2,0,1:T(8,128)(2,1)}, u32[]{:S(2)}, u32[]{:S(2)}) async-start(bf16[64,4,1536]{2,0,1:T(8,128)(2,1)} %copy.52), calls=%async_computation.1 | async-start | bytes 1572864 | tf_op jit(solution)/shard_map/all_to_all | solution.py:110
  13.1 10.5 %copy-start.14 = (s32[1,512]{1,0:T(1,128)S(1)}, s32[1,512]{1,0:T(1,128)}, u32[]{:S(2)}) copy-start(s32[1,512]{1,0:T(1,128)} %param.17) | copy-start | bytes 6148
  13.1 11.2 %copy-start.18 = (bf16[2,1536]{1,0:T(2,128)(2,1)S(1)}, bf16[2,1536]{1,0:T(2,128)(2,1)}, u32[]{:S(2)}) copy-start(bf16[2,1536]{1,0:T(2,128)(2,1)} %param.21) | copy-start | bytes 18436
  20.1 13.8 %all-to-all-start.5 = ((bf16[64,4,1536]{2,0,1:T(8,128)(2,1)}), bf16[64,4,1536]{2,0,1:T(8,128)(2,1)S(1)}, u32[]{:S(2)}, u32[]{:S(2)}) async-start(bf16[64,4,1536]{2,0,1:T(8,128)(2,1)} %copy.61), calls=%async_computation.5 | async-start | bytes 1572864 | tf_op jit(solution)/shard_map/all_to_all | solution.py:110
  24.9 21.0 %copy-start.25 = (f32[2,512]{1,0:T(2,128)S(1)}, f32[2,512]{1,0:T(2,128)}, u32[]{:S(2)}) copy-start(f32[2,512]{1,0:T(2,128)} %param.25) | copy-start | bytes 12292
  33.9 16.6 %all-to-all-start.2 = ((bf16[64,4,2048]{2,0,1:T(8,128)(2,1)}), bf16[64,4,2048]{2,0,1:T(8,128)(2,1)S(1)}, u32[]{:S(2)}, u32[]{:S(2)}) async-start(bf16[64,4,2048]{2,0,1:T(8,128)(2,1)} %copy.58), calls=%async_computation.2 | async-start | bytes 2097152 | tf_op jit(solution)/shard_map/all_to_all | solution.py:110
  45.8 12.7 %copy-start.15 = (bf16[2,2048]{1,0:T(2,128)(2,1)S(1)}, bf16[2,2048]{1,0:T(2,128)(2,1)}, u32[]{:S(2)}) copy-start(bf16[2,2048]{1,0:T(2,128)(2,1)} %param.22) | copy-start | bytes 24580
  45.9 11.7 %collective-permute-start = (bf16[256,1536]{1,0:T(8,128)(2,1)}, bf16[256,1536]{1,0:T(8,128)(2,1)}, u32[]{:S(2)}, u32[]{:S(2)}) collective-permute-start(bf16[256,1536]{1,0:T(8,128)(2,1)} %bitcast.9), channel_id=1, source_target_pairs={{0,4},{4,8},{8,12},{12,16},{16,20},{20,24},{24,28},{28,0},{1,5},{5... | collective-permute-start | bytes 2359304 | tf_op jit(solution)/shard_map/ppermute | solution.py:25
  50.5 44.4 %copy-start.5 = (bf16[64,4,2048]{2,0,1:T(8,128)(2,1)}, bf16[64,4,2048]{2,0,1:T(8,128)(2,1)S(1)}, u32[]{:S(2)}) copy-start(bf16[64,4,2048]{2,0,1:T(8,128)(2,1)S(1)} %all-to-all-done.2) | copy-start | bytes 3145732
  53.4 28.0 %all-to-all-start = ((bf16[4,512,512]{1,2,0:T(8,128)(2,1)}), bf16[4,512,512]{1,2,0:T(8,128)(2,1)S(1)}, u32[]{:S(2)}, u32[]{:S(2)}) async-start(bf16[4,512,512]{1,2,0:T(8,128)(2,1)} %broadcast_in_dim.43), calls=%async_computation | async-start | bytes 4194304 | tf_op jit(solution)/shard_map/all_to_all | solution.py:96
  57.7 11.7 %collective-permute-start.1 = (bf16[256,1536]{1,0:T(8,128)(2,1)}, bf16[256,1536]{1,0:T(8,128)(2,1)}, u32[]{:S(2)}, u32[]{:S(2)}) collective-permute-start(bf16[256,1536]{1,0:T(8,128)(2,1)} %collective-permute-done), channel_id=1, source_target_pairs={{0,4},{4,8},{8,12},{12,16},{16,20},{20,24},{24,28},{28,0},{1,5},{5... | collective-permute-start | bytes 2359304 | tf_op jit(solution)/shard_map/ppermute | solution.py:25
  69.4 19.3 %collective-permute-start.2 = (bf16[256,1536]{1,0:T(8,128)(2,1)}, bf16[256,1536]{1,0:T(8,128)(2,1)}, u32[]{:S(2)}, u32[]{:S(2)}) collective-permute-start(bf16[256,1536]{1,0:T(8,128)(2,1)} %collective-permute-done.1), channel_id=1, source_target_pairs={{0,4},{4,8},{8,12},{12,16},{16,20},{20,24},{24,28},{28,0},{1,5},{5... | collective-permute-start | bytes 2359304 | tf_op jit(solution)/shard_map/ppermute | solution.py:25
  71.2 23.7 %collective-permute-start.4 = (bf16[256,1536]{1,0:T(8,128)(2,1)}, bf16[256,1536]{1,0:T(8,128)(2,1)}, u32[]{:S(2)}, u32[]{:S(2)}) collective-permute-start(bf16[256,1536]{1,0:T(8,128)(2,1)} %bitcast.9), channel_id=1, source_target_pairs={{4,0},{8,4},{12,8},{16,12},{20,16},{24,20},{28,24},{0,28},{5,1},{9... | collective-permute-start | bytes 2359304 | tf_op jit(solution)/shard_map/ppermute | solution.py:28
  72.9 25.8 %collective-permute-start.14 = (bf16[256,1536]{1,0:T(8,128)(2,1)}, bf16[256,1536]{1,0:T(8,128)(2,1)}, u32[]{:S(2)}, u32[]{:S(2)}) collective-permute-start(bf16[256,1536]{1,0:T(8,128)(2,1)} %bitcast.267), channel_id=1, source_target_pairs={{0,4},{4,8},{8,12},{12,16},{16,20},{20,24},{24,28},{28,0},{1,5},{5... | collective-permute-start | bytes 2359304 | tf_op jit(solution)/shard_map/ppermute | solution.py:25
  75.0 79.1 %collective-permute-start.18 = (bf16[256,1536]{1,0:T(8,128)(2,1)}, bf16[256,1536]{1,0:T(8,128)(2,1)}, u32[]{:S(2)}, u32[]{:S(2)}) collective-permute-start(bf16[256,1536]{1,0:T(8,128)(2,1)} %bitcast.268), channel_id=1, source_target_pairs={{4,0},{8,4},{12,8},{16,12},{20,16},{24,20},{28,24},{0,28},{5,1},{9... | collective-permute-start | bytes 2359304 | tf_op jit(solution)/shard_map/ppermute | solution.py:28
  75.0 83.3 %collective-permute-start.7 = (bf16[256,2048]{1,0:T(8,128)(2,1)S(1)}, bf16[256,2048]{1,0:T(8,128)(2,1)}, u32[]{:S(2)}, u32[]{:S(2)}) collective-permute-start(bf16[256,2048]{1,0:T(8,128)(2,1)S(1)} %bitcast.264), channel_id=1, source_target_pairs={{0,4},{4,8},{8,12},{12,16},{16,20},{20,24},{24,28},{28,0},{1,5},{5... | collective-permute-start | bytes 3145736 | tf_op jit(solution)/shard_map/ppermute | solution.py:25
  81.4 72.8 %all-to-all-start.6 = ((bf16[64,4,2048]{2,0,1:T(8,128)(2,1)}), bf16[64,4,2048]{2,0,1:T(8,128)(2,1)}, u32[]{:S(2)}, u32[]{:S(2)}) async-start(bf16[64,4,2048]{2,0,1:T(8,128)(2,1)} %copy.67), calls=%async_computation.6 | async-start | bytes 2097152 | tf_op jit(solution)/shard_map/all_to_all | solution.py:110
  88.7 52.4 %collective-permute-start.3 = (bf16[256,1536]{1,0:T(8,128)(2,1)}, bf16[256,1536]{1,0:T(8,128)(2,1)S(1)}, u32[]{:S(2)}, u32[]{:S(2)}) collective-permute-start(bf16[256,1536]{1,0:T(8,128)(2,1)} %collective-permute-done.2), channel_id=1, source_target_pairs={{0,4},{4,8},{8,12},{12,16},{16,20},{20,24},{24,28},{28,0},{1,5},{5... | collective-permute-start | bytes 2359304 | tf_op jit(solution)/shard_map/ppermute | solution.py:25
  94.9 65.5 %collective-permute-start.11 = (bf16[256,2048]{1,0:T(8,128)(2,1)S(1)}, bf16[256,2048]{1,0:T(8,128)(2,1)}, u32[]{:S(2)}, u32[]{:S(2)}) collective-permute-start(bf16[256,2048]{1,0:T(8,128)(2,1)S(1)} %bitcast.265), channel_id=1, source_target_pairs={{4,0},{8,4},{12,8},{16,12},{20,16},{24,20},{28,24},{0,28},{5,1},{9... | collective-permute-start | bytes 3145736 | tf_op jit(solution)/shard_map/ppermute | solution.py:28
  98.7 61.7 %collective-permute-start.5 = (bf16[256,1536]{1,0:T(8,128)(2,1)}, bf16[256,1536]{1,0:T(8,128)(2,1)S(1)}, u32[]{:S(2)}, u32[]{:S(2)}) collective-permute-start(bf16[256,1536]{1,0:T(8,128)(2,1)} %collective-permute-done.4), channel_id=1, source_target_pairs={{4,0},{8,4},{12,8},{16,12},{20,16},{24,20},{28,24},{0,28},{5,1},{9... | collective-permute-start | bytes 2359304 | tf_op jit(solution)/shard_map/ppermute | solution.py:28
  141.1 21.7 %collective-permute-start.15 = (bf16[256,1536]{1,0:T(8,128)(2,1)}, bf16[256,1536]{1,0:T(8,128)(2,1)}, u32[]{:S(2)}, u32[]{:S(2)}) collective-permute-start(bf16[256,1536]{1,0:T(8,128)(2,1)} %collective-permute-done.14), channel_id=1, source_target_pairs={{0,4},{4,8},{8,12},{12,16},{16,20},{20,24},{24,28},{28,0},{1,5},{5... | collective-permute-start | bytes 2359304 | tf_op jit(solution)/shard_map/ppermute | solution.py:25
  154.2 22.4 %collective-permute-start.21 = (bf16[256,2048]{1,0:T(8,128)(2,1)}, bf16[256,2048]{1,0:T(8,128)(2,1)}, u32[]{:S(2)}, u32[]{:S(2)}) collective-permute-start(bf16[256,2048]{1,0:T(8,128)(2,1)} %bitcast.98), channel_id=1, source_target_pairs={{0,4},{4,8},{8,12},{12,16},{16,20},{20,24},{24,28},{28,0},{1,5},{5... | collective-permute-start | bytes 3145736 | tf_op jit(solution)/shard_map/ppermute | solution.py:25
  158.3 24.8 %collective-permute-start.25 = (bf16[256,2048]{1,0:T(8,128)(2,1)}, bf16[256,2048]{1,0:T(8,128)(2,1)}, u32[]{:S(2)}, u32[]{:S(2)}) collective-permute-start(bf16[256,2048]{1,0:T(8,128)(2,1)} %bitcast.98), channel_id=1, source_target_pairs={{4,0},{8,4},{12,8},{16,12},{20,16},{24,20},{28,24},{0,28},{5,1},{9... | collective-permute-start | bytes 3145736 | tf_op jit(solution)/shard_map/ppermute | solution.py:28
  160.4 38.7 %collective-permute-start.19 = (bf16[256,1536]{1,0:T(8,128)(2,1)}, bf16[256,1536]{1,0:T(8,128)(2,1)S(1)}, u32[]{:S(2)}, u32[]{:S(2)}) collective-permute-start(bf16[256,1536]{1,0:T(8,128)(2,1)} %collective-permute-done.18), channel_id=1, source_target_pairs={{4,0},{8,4},{12,8},{16,12},{20,16},{24,20},{28,24},{0,28},{5,1},{9... | collective-permute-start | bytes 2359304 | tf_op jit(solution)/shard_map/ppermute | solution.py:28
  160.4 55.4 %collective-permute-start.6 = (bf16[256,1536]{1,0:T(8,128)(2,1)S(1)}, bf16[256,1536]{1,0:T(8,128)(2,1)S(1)}, u32[]{:S(2)}, u32[]{:S(2)}) collective-permute-start(bf16[256,1536]{1,0:T(8,128)(2,1)S(1)} %collective-permute-done.5), channel_id=1, source_target_pairs={{4,0},{8,4},{12,8},{16,12},{20,16},{24,20},{28,24},{0,28},{5,1},{9... | collective-permute-start | bytes 2359304 | tf_op jit(solution)/shard_map/ppermute | solution.py:28
  162.8 62.9 %collective-permute-start.16 = (bf16[256,1536]{1,0:T(8,128)(2,1)}, bf16[256,1536]{1,0:T(8,128)(2,1)}, u32[]{:S(2)}, u32[]{:S(2)}) collective-permute-start(bf16[256,1536]{1,0:T(8,128)(2,1)} %collective-permute-done.15), channel_id=1, source_target_pairs={{0,4},{4,8},{8,12},{12,16},{16,20},{20,24},{24,28},{28,0},{1,5},{5... | collective-permute-start | bytes 2359304 | tf_op jit(solution)/shard_map/ppermute | solution.py:25
  176.5 59.5 %collective-permute-start.8 = (bf16[256,2048]{1,0:T(8,128)(2,1)}, bf16[256,2048]{1,0:T(8,128)(2,1)}, u32[]{:S(2)}, u32[]{:S(2)}) collective-permute-start(bf16[256,2048]{1,0:T(8,128)(2,1)} %collective-permute-done.7), channel_id=1, source_target_pairs={{0,4},{4,8},{8,12},{12,16},{16,20},{20,24},{24,28},{28,0},{1,5},{5... | collective-permute-start | bytes 3145736 | tf_op jit(solution)/shard_map/ppermute | solution.py:25
  183.1 55.3 %collective-permute-start.12 = (bf16[256,2048]{1,0:T(8,128)(2,1)}, bf16[256,2048]{1,0:T(8,128)(2,1)}, u32[]{:S(2)}, u32[]{:S(2)}) collective-permute-start(bf16[256,2048]{1,0:T(8,128)(2,1)} %collective-permute-done.11), channel_id=1, source_target_pairs={{4,0},{8,4},{12,8},{16,12},{20,16},{24,20},{28,24},{0,28},{5,1},{9... | collective-permute-start | bytes 3145736 | tf_op jit(solution)/shard_map/ppermute | solution.py:28
  199.1 19.1 %copy-start.12 = (bf16[256,1536]{1,0:T(8,128)(2,1)}, bf16[256,1536]{1,0:T(8,128)(2,1)S(1)}, u32[]{:S(2)}) copy-start(bf16[256,1536]{1,0:T(8,128)(2,1)S(1)} %collective-permute-done.19) | copy-start | bytes 2359300
  199.1 40.2 %collective-permute-start.22 = (bf16[256,2048]{1,0:T(8,128)(2,1)}, bf16[256,2048]{1,0:T(8,128)(2,1)}, u32[]{:S(2)}, u32[]{:S(2)}) collective-permute-start(bf16[256,2048]{1,0:T(8,128)(2,1)} %collective-permute-done.21), channel_id=1, source_target_pairs={{0,4},{4,8},{8,12},{12,16},{16,20},{20,24},{24,28},{28,0},{1,5},{5... | collective-permute-start | bytes 3145736 | tf_op jit(solution)/shard_map/ppermute | solution.py:25
  215.9 45.0 %collective-permute-start.26 = (bf16[256,2048]{1,0:T(8,128)(2,1)}, bf16[256,2048]{1,0:T(8,128)(2,1)}, u32[]{:S(2)}, u32[]{:S(2)}) collective-permute-start(bf16[256,2048]{1,0:T(8,128)(2,1)} %collective-permute-done.25), channel_id=1, source_target_pairs={{4,0},{8,4},{12,8},{16,12},{20,16},{24,20},{28,24},{0,28},{5,1},{9... | collective-permute-start | bytes 3145736 | tf_op jit(solution)/shard_map/ppermute | solution.py:28
  225.7 36.1 %collective-permute-start.17 = (bf16[256,1536]{1,0:T(8,128)(2,1)}, bf16[256,1536]{1,0:T(8,128)(2,1)}, u32[]{:S(2)}, u32[]{:S(2)}) collective-permute-start(bf16[256,1536]{1,0:T(8,128)(2,1)} %collective-permute-done.16), channel_id=1, source_target_pairs={{0,4},{4,8},{8,12},{12,16},{16,20},{20,24},{24,28},{28,0},{1,5},{5... | collective-permute-start | bytes 2359304 | tf_op jit(solution)/shard_map/ppermute | solution.py:25
  236.0 35.4 %copy-start.8 = (bf16[64,4,1536]{2,0,1:T(8,128)(2,1)S(1)}, bf16[64,4,1536]{2,0,1:T(8,128)(2,1)}, u32[]{:S(2)}) copy-start(bf16[64,4,1536]{2,0,1:T(8,128)(2,1)} %copy-done.7) | copy-start | bytes 2359300
  236.1 49.4 %collective-permute-start.20 = (bf16[256,1536]{1,0:T(8,128)(2,1)}, bf16[256,1536]{1,0:T(8,128)(2,1)}, u32[]{:S(2)}, u32[]{:S(2)}) collective-permute-start(bf16[256,1536]{1,0:T(8,128)(2,1)} %copy-done.12), channel_id=1, source_target_pairs={{4,0},{8,4},{12,8},{16,12},{20,16},{24,20},{28,24},{0,28},{5,1},{9... | collective-permute-start | bytes 2359304 | tf_op jit(solution)/shard_map/ppermute | solution.py:28
  238.4 49.1 %collective-permute-start.9 = (bf16[256,2048]{1,0:T(8,128)(2,1)}, bf16[256,2048]{1,0:T(8,128)(2,1)}, u32[]{:S(2)}, u32[]{:S(2)}) collective-permute-start(bf16[256,2048]{1,0:T(8,128)(2,1)} %collective-permute-done.8), channel_id=1, source_target_pairs={{0,4},{4,8},{8,12},{12,16},{16,20},{20,24},{24,28},{28,0},{1,5},{5... | collective-permute-start | bytes 3145736 | tf_op jit(solution)/shard_map/ppermute | solution.py:25
  239.3 98.4 %collective-permute-start.13 = (bf16[256,2048]{1,0:T(8,128)(2,1)}, bf16[256,2048]{1,0:T(8,128)(2,1)}, u32[]{:S(2)}, u32[]{:S(2)}) collective-permute-start(bf16[256,2048]{1,0:T(8,128)(2,1)} %collective-permute-done.12), channel_id=1, source_target_pairs={{4,0},{8,4},{12,8},{16,12},{20,16},{24,20},{28,24},{0,28},{5,1},{9... | collective-permute-start | bytes 3145736 | tf_op jit(solution)/shard_map/ppermute | solution.py:28
  260.9 45.6 %collective-permute-start.23 = (bf16[256,2048]{1,0:T(8,128)(2,1)}, bf16[256,2048]{1,0:T(8,128)(2,1)}, u32[]{:S(2)}, u32[]{:S(2)}) collective-permute-start(bf16[256,2048]{1,0:T(8,128)(2,1)} %collective-permute-done.22), channel_id=1, source_target_pairs={{0,4},{4,8},{8,12},{12,16},{16,20},{20,24},{24,28},{28,0},{1,5},{5... | collective-permute-start | bytes 3145736 | tf_op jit(solution)/shard_map/ppermute | solution.py:25
  261.8 160.4 %collective-permute-start.27 = (bf16[256,2048]{1,0:T(8,128)(2,1)}, bf16[256,2048]{1,0:T(8,128)(2,1)}, u32[]{:S(2)}, u32[]{:S(2)}) collective-permute-start(bf16[256,2048]{1,0:T(8,128)(2,1)} %collective-permute-done.26), channel_id=1, source_target_pairs={{4,0},{8,4},{12,8},{16,12},{20,16},{24,20},{28,24},{0,28},{5,1},{9... | collective-permute-start | bytes 3145736 | tf_op jit(solution)/shard_map/ppermute | solution.py:28
  287.5 35.1 %collective-permute-start.10 = (bf16[256,2048]{1,0:T(8,128)(2,1)}, bf16[256,2048]{1,0:T(8,128)(2,1)}, u32[]{:S(2)}, u32[]{:S(2)}) collective-permute-start(bf16[256,2048]{1,0:T(8,128)(2,1)} %collective-permute-done.9), channel_id=1, source_target_pairs={{0,4},{4,8},{8,12},{12,16},{16,20},{20,24},{24,28},{28,0},{1,5},{5... | collective-permute-start | bytes 3145736 | tf_op jit(solution)/shard_map/ppermute | solution.py:25
  306.5 25.5 %copy-start.6 = (bf16[64,4,2048]{2,0,1:T(8,128)(2,1)S(1)}, bf16[64,4,2048]{2,0,1:T(8,128)(2,1)}, u32[]{:S(2)}) copy-start(bf16[64,4,2048]{2,0,1:T(8,128)(2,1)} %copy-done.5) | copy-start | bytes 3145732
  306.5 77.7 %collective-permute-start.24 = (bf16[256,2048]{1,0:T(8,128)(2,1)}, bf16[256,2048]{1,0:T(8,128)(2,1)S(1)}, u32[]{:S(2)}, u32[]{:S(2)}) collective-permute-start(bf16[256,2048]{1,0:T(8,128)(2,1)} %collective-permute-done.23), channel_id=1, source_target_pairs={{0,4},{4,8},{8,12},{12,16},{16,20},{20,24},{24,28},{28,0},{1,5},{5... | collective-permute-start | bytes 3145736 | tf_op jit(solution)/shard_map/ppermute | solution.py:25
  380.0 29.3 %all-to-all-start.3 = ((bf16[4,512,512]{2,1,0:T(8,128)(2,1)}), bf16[4,512,512]{2,1,0:T(8,128)(2,1)S(1)}, u32[]{:S(2)}, u32[]{:S(2)}) async-start(bf16[4,512,512]{2,1,0:T(8,128)(2,1)} %bitcast.251), calls=%async_computation.3 | async-start | bytes 4194304 | tf_op jit(solution)/shard_map/all_to_all | solution.py:96
  387.6 22.1 %copy-start.11 = (bf16[1,512,512]{2,1,0:T(8,128)(2,1)S(1)}, bf16[1,512,512]{2,1,0:T(8,128)(2,1)}, u32[]{:S(2)}) copy-start(bf16[1,512,512]{2,1,0:T(8,128)(2,1)} %param.16) | copy-start | bytes 1572868
  387.6 22.1 %copy-start.20 = (f32[1,512]{1,0:T(1,128)S(1)}, f32[1,512]{1,0:T(1,128)}, u32[]{:S(2)}) copy-start(f32[1,512]{1,0:T(1,128)} %get-tuple-element.44) | copy-start | bytes 6148
  411.6 29.8 %all-to-all-start.4 = ((bf16[4,512,512]{1,2,0:T(8,128)(2,1)}), bf16[4,512,512]{1,2,0:T(8,128)(2,1)S(1)}, u32[]{:S(2)}, u32[]{:S(2)}) async-start(bf16[4,512,512]{1,2,0:T(8,128)(2,1)} %broadcast_in_dim.52), calls=%async_computation.4 | async-start | bytes 4194304 | tf_op jit(solution)/shard_map/all_to_all | solution.py:96
  480.5 26.3 %copy-start.13 = (bf16[2,256,512]{2,1,0:T(8,128)(2,1)S(1)}, bf16[2,256,512]{2,1,0:T(8,128)(2,1)}, u32[]{:S(2)}) copy-start(bf16[2,256,512]{2,1,0:T(8,128)(2,1)} %convolution_convert_fusion) | copy-start | bytes 1572868
  511.1 28.8 %copy-start.4 = (bf16[1,512,512]{2,1,0:T(8,128)(2,1)S(1)}, bf16[1,512,512]{2,1,0:T(8,128)(2,1)}, u32[]{:S(2)}) copy-start(bf16[1,512,512]{2,1,0:T(8,128)(2,1)} %copy-done.3) | copy-start | bytes 1572868
  511.1 28.8 %copy-start.19 = (f32[1,512]{1,0:T(1,128)S(1)}, f32[1,512]{1,0:T(1,128)}, u32[]{:S(2)}) copy-start(f32[1,512]{1,0:T(1,128)} %get-tuple-element.43) | copy-start | bytes 6148
  (14 other events, 67.7 us)
